TPU v7x, 512 devices: a whole 4x8x8 slice. The times are simulated.
512 devices in a mesh: sub: 8 (over x, core), seq: 8 (over y), exp: 8 (over z).
Axes of the slice: x: 4, y: 8, z: 8, core: 2. Of those that a mesh axis runs over, the one named last changes fastest.
Arguments:
- node_features: bfloat16 [64, 1536, 1024], P(('sub', 'exp'), 'seq'), parts along dimension 0, may hold values from -24 to 24
- block_mask: int32 [64, 12, 12], P(('sub', 'exp')), parts along dimension 0, may hold values from 0 to 1, as said below
- w_qkv: bfloat16 [1024, 3072], P('exp', 'seq'), may hold values from -4 to 4
- w_out: bfloat16 [1024, 1024], P('seq', 'exp'), may hold values from -0.1875 to 0.1875
- norm_gain: float32 [1024], replicated, may hold values from 0.5 to 1.5
- routes: int32 [64, 1536, 2], P(('sub', 'exp'), 'seq'), parts along dimension 0, may hold values from 0 to 63, all different within a row; in each aligned block of 192 rows (0 to 191, 192 to 383, ..., all dimensions but the last counted through in order) at most 12 rows name the same one
- gates: float32 [64, 1536, 2], P(('sub', 'exp'), 'seq'), parts along dimension 0, may hold values from 0.1 to 1
- w_gate_up: bfloat16 [64, 1024, 1024], P(('seq', 'exp')), may hold values from -0.1875 to 0.1875
- w_down: bfloat16 [64, 512, 1024], P(('seq', 'exp')), may hold values from -0.25 to 0.25
Outputs:
- layer_out: bfloat16 [64, 1536, 1024], P(('sub', 'exp'), 'seq'), parts along dimension 0
There are 8 independent parts, one for each index of `sub`. A program takes and returns all parts, laid end to end along the dimension named above; an argument that names none is the same for every part. Nothing has to cross between parts.
Inputs may be any that keep to these rules, and one draw needn't show every extreme that they name: In each aligned block of 192 rows (one device's nodes, subgraphs then nodes in order) no expert is named by more than 12 of the rows' routes, a bound that some block reaches; the 2 experts of a node differ. `block_mask`: the diagonal blocks are 1.
All inputs are finite; a program needn't handle non-finite values.
Results may differ from a plain program's by a relative error of at most 0.0065.
The roundings to bfloat16 on the way count: a program that leaves them out, or rounds other values in their place, can miss the bound.
Values may be sent and summed in bfloat16 or wider, within the bound.
No kernel may reach another device: no remote copies, remote signals or barrier semaphores. Data moves between devices by JAX's collectives and lax.ppermute only.
A program may use at most 64 MiB of HBM per device.

v0:
```python
import math
import jax
import jax.numpy as jnp
from jax import lax
from jax.sharding import PartitionSpec as P

HEAD_DIM = 64
TOP = 2
BLOCK = 128


def per_device(
    node_features, block_mask, w_qkv, w_out, norm_gain, routes, gates, w_gate_up, w_down
):
    feats = node_features[0]
    node_dev, width = feats.shape
    seq_count = lax.axis_size("seq")
    exp_count = lax.axis_size("exp")
    experts = seq_count * exp_count * w_gate_up.shape[0]
    head_cols = w_qkv.shape[1]
    cols_slice = lax.all_gather(w_qkv, "exp", axis=0, tiled=True)
    out_rows = lax.all_gather(w_out[None], "exp", axis=0, tiled=True)
    out_all = lax.all_gather(out_rows[None], "seq", axis=0, tiled=True)
    me = lax.axis_index("seq")
    right = [(i, (i + 1) % seq_count) for i in range(seq_count)]
    left = [(i, (i - 1) % seq_count) for i in range(seq_count)]
    relative = [None] * seq_count
    relative[0] = feats
    moving_r, moving_l = (feats, feats)
    for step in range(1, seq_count // 2 + 1):
        moving_r = lax.ppermute(moving_r, "seq", right)
        relative[(seq_count - step) % seq_count] = moving_r
        if step < seq_count - step:
            moving_l = lax.ppermute(moving_l, "seq", left)
            relative[step] = moving_l
    stacked = jnp.stack(relative)
    order = (jnp.arange(seq_count, dtype=jnp.int32) - me) % seq_count
    gathered = jnp.take(stacked, order, axis=0).reshape(seq_count * node_dev, width)
    projected = jnp.dot(gathered, cols_slice, preferred_element_type=jnp.float32).astype(
        jnp.bfloat16
    )
    nodes = projected.shape[0]
    heads_here = head_cols // (3 * HEAD_DIM)
    split = projected.reshape(nodes, heads_here, 3, HEAD_DIM)
    query = split[:, :, 0]
    keys = split[:, :, 1]
    values = split[:, :, 2]
    col_mask = jnp.repeat(block_mask[0], BLOCK, axis=1) > 0
    span = math.gcd(nodes, 512)
    scale = 1.0 / math.sqrt(HEAD_DIM)

    def attend(index):
        start = index * span
        rows_query = lax.dynamic_slice_in_dim(query, start, span, 0)
        rows_mask = lax.dynamic_slice_in_dim(col_mask, start // BLOCK, span // BLOCK, 0)
        allowed = jnp.repeat(rows_mask, BLOCK, axis=0)
        scores = (
            jnp.einsum("qhd,khd->hqk", rows_query, keys, preferred_element_type=jnp.float32) * scale
        )
        scores = jnp.where(allowed[None], scores, -1e30)
        top = jnp.max(scores, axis=-1, keepdims=True)
        weights = jnp.exp(scores - top)
        probs = (weights / jnp.sum(weights, axis=-1, keepdims=True)).astype(jnp.bfloat16)
        return jnp.einsum("hqk,khd->qhd", probs, values, preferred_element_type=jnp.float32).astype(
            jnp.bfloat16
        )

    blocks = lax.map(attend, jnp.arange(nodes // span, dtype=jnp.int32))
    attended = blocks.reshape(nodes, heads_here * HEAD_DIM)
    node_attended = lax.all_to_all(attended, "seq", split_axis=0, concat_axis=1, tiled=True)
    out_tiles = out_all
    attn_out = jnp.einsum(
        "nsk,sekc->nec",
        node_attended.reshape(node_dev, seq_count, w_out.shape[0]),
        out_tiles,
        preferred_element_type=jnp.float32,
    )
    mixed = feats.astype(jnp.float32) + attn_out.reshape(node_dev, width)
    mean_square = jnp.mean(mixed * mixed, axis=-1, keepdims=True)
    normed = (mixed * lax.rsqrt(mean_square + 1e-06) * norm_gain).astype(jnp.bfloat16)
    capacity = 2 * TOP * node_dev // experts
    pair_routes = routes[0].reshape(node_dev * TOP)
    onehot = (pair_routes[:, None] == jnp.arange(experts, dtype=jnp.int32)).astype(jnp.int32)
    earlier = jnp.cumsum(onehot, axis=0, dtype=jnp.int32) - onehot
    slots = jnp.sum(earlier * onehot, axis=1, dtype=jnp.int32)
    position = pair_routes * capacity + slots
    outgoing = (
        jnp.zeros((experts * capacity, width), jnp.bfloat16)
        .at[position]
        .set(jnp.repeat(normed, TOP, axis=0))
    )
    outgoing = outgoing.reshape(experts, capacity, width)
    hidden_units = w_down.shape[1]
    received = lax.all_to_all(outgoing, ("seq", "exp"), split_axis=0, concat_axis=0, tiled=True)
    sources, items, columns = received.shape
    flat_rows = received.reshape(sources * items, columns)
    both = jnp.dot(flat_rows, w_gate_up[0], preferred_element_type=jnp.float32)
    hidden = (jax.nn.silu(both[:, :hidden_units]) * both[:, hidden_units:]).astype(jnp.bfloat16)
    result = jnp.dot(hidden, w_down[0], preferred_element_type=jnp.float32).astype(jnp.bfloat16)
    processed = result.reshape(sources, items, columns)
    returned = lax.all_to_all(
        processed, ("seq", "exp"), split_axis=0, concat_axis=0, tiled=True
    ).reshape(experts * capacity, width)
    picked = returned[position].astype(jnp.float32).reshape(node_dev, TOP, width)
    expert_sum = jnp.sum(picked * gates[0][:, :, None], axis=1)
    return (mixed + expert_sum).astype(jnp.bfloat16)[None]


def solution(mesh):
    in_specs = (
        P(("sub", "exp"), "seq", None),
        P(("sub", "exp"), None, None),
        P("exp", "seq"),
        P("seq", "exp"),
        P(),
        P(("sub", "exp"), "seq", None),
        P(("sub", "exp"), "seq", None),
        P(("seq", "exp"), None, None),
        P(("seq", "exp"), None, None),
    )
    out_specs = P(("sub", "exp"), "seq", None)
    return jax.shard_map(
        per_device, mesh=mesh, in_specs=in_specs, out_specs=out_specs, check_vma=False
    )
```

profile of v0, /device:TPU:26, one launch (start us, length us, event | category | flops | bytes accessed | tf_op | source)
XLA Modules:
  0.0 344.0 jit_solution(16411049561203123971)
XLA Ops:
  6.5 2.5 collective-permute-start
  9.0 4.7 %collective-permute-start.3 = (bf16[192,1024]{1,0:T(8,128)(2,1)}, bf16[192,1024]{1,0:T(8,128)(2,1)S(1)}, u32[]{:S(2)}, u32[]{:S(2)}) collective-permute-start(bf16[192,1024]{1,0:T(8,128)(2,1)} %bitcast.114), channel_id=1, source_target_pairs={{0,8},{8,16},{16,24},{24,32},{32,40},{40,48},{48,56},{56,0},{1,9},... | collective-permute-start | bytes 1179656 | tf_op jit(solution)/shard_map/ppermute | solution.py:31
  13.7 33.4 %all-gather = bf16[1024,128]{1,0:T(8,128)(2,1)} all-gather(bf16[128,128]{1,0:T(8,128)(2,1)} %param.14), channel_id=2, replica_groups=mesh['sub'=8,'seq'=8,'exp'=8] {'exp'}, dimensions={0}, use_global_device_ids=true | all-gather | bytes 294912 | tf_op jit(solution)/shard_map/all_gather | solution.py:22
  47.1 26.4 %all_gather.9 = bf16[1024,384]{1,0:T(8,128)(2,1)S(1)} all-gather(bf16[128,384]{1,0:T(8,128)(2,1)} %param.13), channel_id=1, replica_groups=mesh['sub'=8,'seq'=8,'exp'=8] {'exp'}, dimensions={0}, use_global_device_ids=true | all-gather | bytes 884736 | tf_op jit(solution)/shard_map/all_gather | solution.py:21
  73.5 3.3 collective-permute-start.4
  77.6 2.5 collective-permute-start.1
  80.1 11.0 %collective-permute-done.4 = bf16[192,1024]{1,0:T(8,128)(2,1)} collective-permute-done((bf16[192,1024]{1,0:T(8,128)(2,1)S(1)}, bf16[192,1024]{1,0:T(8,128)(2,1)}, u32[]{:S(2)}, u32[]{:S(2)}) %collective-permute-start.4) | collective-permute-done | bytes 393248 | tf_op jit(solution)/shard_map/ppermute | solution.py:31
  91.1 4.7 %collective-permute-start.5 = (bf16[192,1024]{1,0:T(8,128)(2,1)}, bf16[192,1024]{1,0:T(8,128)(2,1)}, u32[]{:S(2)}, u32[]{:S(2)}) collective-permute-start(bf16[192,1024]{1,0:T(8,128)(2,1)} %collective-permute-done.4), channel_id=1, source_target_pairs={{0,8},{8,16},{16,24},{24,32},{32,40},{40,48},{48,56},{56,0},{1,9},... | collective-permute-start | bytes 1179656 | tf_op jit(solution)/shard_map/ppermute | solution.py:31
  97.3 1.8 constant_dynamic-update-slice_fusion
  99.0 1.9 collective-permute-start.2
  100.9 1.8 bitcast_dynamic-update-slice_fusion.6
  102.7 2.4 collective-permute-done.5
  105.1 5.6 %collective-permute-start.6 = (bf16[192,1024]{1,0:T(8,128)(2,1)}, bf16[192,1024]{1,0:T(8,128)(2,1)S(1)}, u32[]{:S(2)}, u32[]{:S(2)}) collective-permute-start(bf16[192,1024]{1,0:T(8,128)(2,1)} %collective-permute-done.5), channel_id=1, source_target_pairs={{0,8},{8,16},{16,24},{24,32},{32,40},{40,48},{48,56},{56,0},{1,9},... | collective-permute-start | bytes 1179656 | tf_op jit(solution)/shard_map/ppermute | solution.py:31
  110.7 1.8 bitcast_dynamic-update-slice_fusion.5
  113.3 3.0 collective-permute-done.6
  117.1 1.8 bitcast_dynamic-update-slice_fusion.2
  118.9 1.8 bitcast_dynamic-update-slice_fusion.1
  121.4 4.3 %gather_fusion = bf16[8,192,1024]{2,1,0:T(8,128)(2,1)} fusion(bf16[8,192,1024]{2,1,0:T(8,128)(2,1)} %bitcast_dynamic-update-slice_fusion, s32[1024]{0:T(1024)S(1)} %pad_clamp_fusion.1), kind=kCustom, calls=%fused_computation | custom fusion | bytes 6291488 | tf_op jit(solution)/shard_map/jit(_take)/gather | solution.py:38
  125.7 2.3 bitcast_select_fusion
  128.1 1.5 convolution_convert_fusion
  130.5 28.2 %while.12 = (s32[]{:T(128)}, bf16[3,512,2,64]{1,3,2,0:T(8,128)(2,1)}, s32[3]{0:T(128)S(1)}, pred[12,1536]{1,0:T(8,128)(4,1)S(1)}, bf16[1536,2,64]{0,2,1:T(8,128)...) while((s32[]{:T(128)}, ...), condition=%wide.region_3.4_spmd, body=%wide.region_0.3_spmd.sunk | while | flops 618205184 | bytes 3959682 | solution.py:68
  132.1 3.4 fusion.75
  135.5 4.4 %fusion.76 = bf16[3,512,2,64]{1,3,2,0:T(8,128)(2,1)} fusion(bf16[3,512,2,64]{1,3,2,0:T(8,128)(2,1)} %get-tuple-element.174, s32[]{:T(128)} %get-tuple-element.173, bf16[1536,2,64]{0,2,1:T(8,128)(2,1)S(1)} %get-tuple-element.194, f32[2,512]{1,0:T(2,128)S(1)} %fusion.75, pred[512,1536]{1,0:T(8,128)(4,1)S(1)} %bitcast.110, ...), kind=kOutput, calls=%fused_computation.14.clone.1 | convolution fusion | flops 410585600 | bytes 1839620 | tf_op jit(solution)/shard_map/while/body/eval_jaxpr/hqk,khd->qhd/dot_general | solution.py:64
  141.5 3.4 fusion.75
  144.9 4.4 %fusion.76 = bf16[3,512,2,64]{1,3,2,0:T(8,128)(2,1)} fusion(bf16[3,512,2,64]{1,3,2,0:T(8,128)(2,1)} %get-tuple-element.174, s32[]{:T(128)} %get-tuple-element.173, bf16[1536,2,64]{0,2,1:T(8,128)(2,1)S(1)} %get-tuple-element.194, f32[2,512]{1,0:T(2,128)S(1)} %fusion.75, pred[512,1536]{1,0:T(8,128)(4,1)S(1)} %bitcast.110, ...), kind=kOutput, calls=%fused_computation.14.clone.1 | convolution fusion | flops 410585600 | bytes 1839620 | tf_op jit(solution)/shard_map/while/body/eval_jaxpr/hqk,khd->qhd/dot_general | solution.py:64
  150.9 3.4 fusion.75
  154.3 4.4 %fusion.76 = bf16[3,512,2,64]{1,3,2,0:T(8,128)(2,1)} fusion(bf16[3,512,2,64]{1,3,2,0:T(8,128)(2,1)} %get-tuple-element.174, s32[]{:T(128)} %get-tuple-element.173, bf16[1536,2,64]{0,2,1:T(8,128)(2,1)S(1)} %get-tuple-element.194, f32[2,512]{1,0:T(2,128)S(1)} %fusion.75, pred[512,1536]{1,0:T(8,128)(4,1)S(1)} %bitcast.110, ...), kind=kOutput, calls=%fused_computation.14.clone.1 | convolution fusion | flops 410585600 | bytes 1839620 | tf_op jit(solution)/shard_map/while/body/eval_jaxpr/hqk,khd->qhd/dot_general | solution.py:64
  158.7 2.2 copy.38
  160.9 1.1 reshape.189
  162.0 8.2 %all-to-all-start = ((bf16[8,192,128]{2,1,0:T(8,128)(2,1)}), bf16[8,192,128]{2,1,0:T(8,128)(2,1)S(1)}, u32[]{:S(2)}, u32[]{:S(2)}) async-start(bf16[8,192,128]{2,1,0:T(8,128)(2,1)} %reshape.189), calls=%async_computation | async-start | bytes 786432 | tf_op jit(solution)/shard_map/all_to_all | solution.py:70
  171.9 3.9 %copy.32 = bf16[8,8,128,128]{2,3,1,0:T(8,128)(2,1)} copy(bf16[8,8,128,128]{3,2,1,0:T(8,128)(2,1)} %bitcast.112) | data formatting | bytes 4194304 | tf_op jit(solution)/shard_map/all_gather | solution.py:23
  175.8 2.9 all-to-all-done
  179.5 2.7 multiply_reduce_fusion.1
  182.3 1.3 broadcast_in_dim.87
  183.6 3.0 reshape.182
  186.6 4.0 %scatter_custom_fusion = bf16[768,1024]{1,0:T(8,128)(2,1)} fusion(s32[384]{0:T(512)S(1)} %fusion.48, bf16[384,1024]{1,0:T(8,128)(2,1)} %reshape.182, bf16[]{:T(256)} %constant.125.clone.1), kind=kCustom, calls=%fused_computation.44 | custom fusion | bytes 1573376 | tf_op jit(solution)/shard_map/scatter | solution.py:90
  190.6 3.6 %reshape.157 = bf16[64,12,1024]{2,1,0:T(8,128)(2,1)} reshape(bf16[768,1024]{1,0:T(8,128)(2,1)} %scatter_custom_fusion) | data formatting | bytes 3145728 | tf_op jit(solution)/shard_map/reshape | solution.py:92
  194.2 52.2 %all_to_all.26 = bf16[64,12,1024]{2,1,0:T(8,128)(2,1)} all-to-all(bf16[64,12,1024]{2,1,0:T(8,128)(2,1)} %reshape.157), channel_id=1, replica_groups=mesh['sub'=8,'seq'=8,'exp'=8] {'seq','exp'}, dimensions={0} | all-to-all | bytes 3145728 | tf_op jit(solution)/shard_map/all_to_all | solution.py:94
  246.3 3.6 %reshape.158 = bf16[768,1024]{1,0:T(8,128)(2,1)} reshape(bf16[64,12,1024]{2,1,0:T(8,128)(2,1)} %all_to_all.26) | data formatting | bytes 3145728 | tf_op jit(solution)/shard_map/reshape | solution.py:96
  250.0 3.3 fusion.33
  253.3 2.2 convolution_convert_fusion.1
  255.4 3.6 %reshape.159 = bf16[64,12,1024]{2,1,0:T(8,128)(2,1)} reshape(bf16[768,1024]{1,0:T(8,128)(2,1)} %convolution_convert_fusion.1) | data formatting | bytes 3145728 | tf_op jit(solution)/shard_map/reshape | solution.py:100
  259.0 9.6 %all-to-all-start.2 = ((bf16[64,12,1024]{2,1,0:T(8,128)(2,1)}), bf16[64,12,1024]{2,1,0:T(8,128)(2,1)}, u32[]{:S(2)}, u32[]{:S(2)}) async-start(bf16[64,12,1024]{2,1,0:T(8,128)(2,1)} %reshape.159), calls=%async_computation.2 | async-start | bytes 4194304 | tf_op jit(solution)/shard_map/all_to_all | solution.py:101
  268.8 52.5 %all-to-all-done.2 = bf16[64,12,1024]{2,1,0:T(8,128)(2,1)} async-done(((bf16[64,12,1024]{2,1,0:T(8,128)(2,1)}), bf16[64,12,1024]{2,1,0:T(8,128)(2,1)}, u32[]{:S(2)}, u32[]{:S(2)}) %all-to-all-start.2) | async-done | bytes 1572896 | tf_op jit(solution)/shard_map/all_to_all | solution.py:101
  321.3 3.6 %reshape.160 = bf16[768,1024]{1,0:T(8,128)(2,1)} reshape(bf16[64,12,1024]{2,1,0:T(8,128)(2,1)} %all-to-all-done.2) | data formatting | bytes 3145728 | tf_op jit(solution)/shard_map/reshape | solution.py:103
  324.9 5.0 %gather_fusion.1 = bf16[384,1024]{1,0:T(8,128)(2,1)} fusion(bf16[768,1024]{1,0:T(8,128)(2,1)} %reshape.160, s32[1024]{0:T(1024)S(1)} %pad_clamp_fusion), kind=kCustom, calls=%fused_computation.1 | custom fusion | bytes 1574400 | tf_op jit(solution)/shard_map/gather | solution.py:104
  329.9 3.0 reshape.161
  332.8 3.4 %multiply_reduce_fusion = f32[192,1024]{1,0:T(8,128)S(1)} fusion(f32[192,2,1024]{2,1,0:T(2,128)} %reshape.161, f32[192,2]{1,0:T(8,128)S(1)} %copy.37), kind=kLoop, calls=%fused_computation.36 | loop fusion | flops 589824 | bytes 2360832 | tf_op jit(solution)/shard_map/reduce_sum | solution.py:105
  (63 shorter events, 11.6 us)
Async XLA Ops:
  6.5 243.4 %copy-start = (bf16[1,1024,1024]{2,1,0:T(8,128)(2,1)S(1)}, bf16[1,1024,1024]{2,1,0:T(8,128)(2,1)}, u32[]{:S(2)}) copy-start(bf16[1,1024,1024]{2,1,0:T(8,128)(2,1)} %param.18) | copy-start | bytes 6291460
  6.5 165.3 %all-gather.4.cloned.1.call-start = ((), (), s32[]{:S(2)}) async-start(), calls=%async_computation.3 | async-start | bytes 2359296 | tf_op jit(solution)/shard_map/all_gather | solution.py:23
  6.5 71.1 %collective-permute-start = (bf16[192,1024]{1,0:T(8,128)(2,1)}, bf16[192,1024]{1,0:T(8,128)(2,1)}, u32[]{:S(2)}, u32[]{:S(2)}) collective-permute-start(bf16[192,1024]{1,0:T(8,128)(2,1)} %bitcast.113), channel_id=1, source_target_pairs={{0,56},{8,0},{16,8},{24,16},{32,24},{40,32},{48,40},{56,48},{1,57}... | collective-permute-start | bytes 1179656 | tf_op jit(solution)/shard_map/ppermute | solution.py:34
  9.0 64.5 %collective-permute-start.3 = (bf16[192,1024]{1,0:T(8,128)(2,1)}, bf16[192,1024]{1,0:T(8,128)(2,1)S(1)}, u32[]{:S(2)}, u32[]{:S(2)}) collective-permute-start(bf16[192,1024]{1,0:T(8,128)(2,1)} %bitcast.114), channel_id=1, source_target_pairs={{0,8},{8,16},{16,24},{24,32},{32,40},{40,48},{48,56},{56,0},{1,9},... | collective-permute-start | bytes 1179656 | tf_op jit(solution)/shard_map/ppermute | solution.py:31
  73.5 17.6 %collective-permute-start.4 = (bf16[192,1024]{1,0:T(8,128)(2,1)S(1)}, bf16[192,1024]{1,0:T(8,128)(2,1)}, u32[]{:S(2)}, u32[]{:S(2)}) collective-permute-start(bf16[192,1024]{1,0:T(8,128)(2,1)S(1)} %collective-permute-done.3), channel_id=1, source_target_pairs={{0,8},{8,16},{16,24},{24,32},{32,40},{40,48},{48,56},{56,0},{1,9},... | collective-permute-start | bytes 1179656 | tf_op jit(solution)/shard_map/ppermute | solution.py:31
  77.6 21.4 %collective-permute-start.1 = (bf16[192,1024]{1,0:T(8,128)(2,1)}, bf16[192,1024]{1,0:T(8,128)(2,1)}, u32[]{:S(2)}, u32[]{:S(2)}) collective-permute-start(bf16[192,1024]{1,0:T(8,128)(2,1)} %collective-permute-done), channel_id=1, source_target_pairs={{0,56},{8,0},{16,8},{24,16},{32,24},{40,32},{48,40},{56,48},{1,57}... | collective-permute-start | bytes 1179656 | tf_op jit(solution)/shard_map/ppermute | solution.py:34
  91.1 14.0 %collective-permute-start.5 = (bf16[192,1024]{1,0:T(8,128)(2,1)}, bf16[192,1024]{1,0:T(8,128)(2,1)}, u32[]{:S(2)}, u32[]{:S(2)}) collective-permute-start(bf16[192,1024]{1,0:T(8,128)(2,1)} %collective-permute-done.4), channel_id=1, source_target_pairs={{0,8},{8,16},{16,24},{24,32},{32,40},{40,48},{48,56},{56,0},{1,9},... | collective-permute-start | bytes 1179656 | tf_op jit(solution)/shard_map/ppermute | solution.py:31
  99.0 13.4 %collective-permute-start.2 = (bf16[192,1024]{1,0:T(8,128)(2,1)}, bf16[192,1024]{1,0:T(8,128)(2,1)S(1)}, u32[]{:S(2)}, u32[]{:S(2)}) collective-permute-start(bf16[192,1024]{1,0:T(8,128)(2,1)} %collective-permute-done.1), channel_id=1, source_target_pairs={{0,56},{8,0},{16,8},{24,16},{32,24},{40,32},{48,40},{56,48},{1,57}... | collective-permute-start | bytes 1179656 | tf_op jit(solution)/shard_map/ppermute | solution.py:34
  105.1 11.2 %collective-permute-start.6 = (bf16[192,1024]{1,0:T(8,128)(2,1)}, bf16[192,1024]{1,0:T(8,128)(2,1)S(1)}, u32[]{:S(2)}, u32[]{:S(2)}) collective-permute-start(bf16[192,1024]{1,0:T(8,128)(2,1)} %collective-permute-done.5), channel_id=1, source_target_pairs={{0,8},{8,16},{16,24},{24,32},{32,40},{40,48},{48,56},{56,0},{1,9},... | collective-permute-start | bytes 1179656 | tf_op jit(solution)/shard_map/ppermute | solution.py:31
  158.7 12.7 %copy-start.3 = (s32[1,192,2]{1,2,0:T(2,128)S(1)}, s32[1,192,2]{1,2,0:T(2,128)}, u32[]{:S(2)}) copy-start(s32[1,192,2]{1,2,0:T(2,128)} %param.16) | copy-start | bytes 4612
  162.0 17.5 %copy-start.1 = (bf16[1,192,1024]{2,1,0:T(8,128)(2,1)S(1)}, bf16[1,192,1024]{2,1,0:T(8,128)(2,1)}, u32[]{:S(2)}) copy-start(bf16[1,192,1024]{2,1,0:T(8,128)(2,1)} %param.11) | copy-start | bytes 1179652
  162.0 16.7 %all-to-all-start = ((bf16[8,192,128]{2,1,0:T(8,128)(2,1)}), bf16[8,192,128]{2,1,0:T(8,128)(2,1)S(1)}, u32[]{:S(2)}, u32[]{:S(2)}) async-start(bf16[8,192,128]{2,1,0:T(8,128)(2,1)} %reshape.189), calls=%async_computation | async-start | bytes 786432 | tf_op jit(solution)/shard_map/all_to_all | solution.py:70
  171.9 10.3 %copy-start.4 = (f32[1024]{0:T(1024)S(1)}, f32[1024]{0:T(1024)}, u32[]{:S(2)}) copy-start(f32[1024]{0:T(1024)} %param.15) | copy-start | bytes 12292
  178.7 0.7 copy-start.2
  250.0 3.3 copy-start.6
  255.4 13.2 %copy-start.5 = (f32[1,192,2]{1,2,0:T(2,128)S(1)}, f32[1,192,2]{1,2,0:T(2,128)}, u32[]{:S(2)}) copy-start(f32[1,192,2]{1,2,0:T(2,128)} %param.17) | copy-start | bytes 4612
  259.0 62.2 %all-to-all-start.2 = ((bf16[64,12,1024]{2,1,0:T(8,128)(2,1)}), bf16[64,12,1024]{2,1,0:T(8,128)(2,1)}, u32[]{:S(2)}, u32[]{:S(2)}) async-start(bf16[64,12,1024]{2,1,0:T(8,128)(2,1)} %reshape.159), calls=%async_computation.2 | async-start | bytes 4194304 | tf_op jit(solution)/shard_map/all_to_all | solution.py:101
Sparse Core Ops, SparseCore 0:
  47.2 43.0 all-gather.3
where the time goes:
time: 346 us; the launch traced here: 344 us
  blocking collectives  112 us (32%)
  waiting for transfers between devices  71.8 us (21%)
  local copies, waits for them, and re-layouts  59.7 us (17%)
  starting transfers between devices  43 us (12%)
  matrix products  33.1 us (10%)
  between operations  13.7 us (4%)
  other arithmetic  8.59 us (2%)
    all_to_all x1, waiting for transfers between devices, per_device(): lax.all_to_all(processed, ('seq', 'exp'), split_axis=0, concat_axis=0, ti...  52.5 us
    all_to_all x1, blocking collectives, per_device(): lax.all_to_all(outgoing, ('seq', 'exp'), split_axis=0, concat_axis=0, til...  52.2 us
    all_gather x1, blocking collectives, per_device(): out_rows = lax.all_gather(w_out[None], 'exp', axis=0, tiled=True)  33.4 us
    all_gather x1, blocking collectives, per_device(): cols_slice = lax.all_gather(w_qkv, 'exp', axis=0, tiled=True)  26.4 us
    ppermute x4, starting transfers between devices, per_device(): moving_r = lax.ppermute(moving_r, 'seq', right)  18.3 us
    ppermute x4, waiting for transfers between devices, per_device(): moving_r = lax.ppermute(moving_r, 'seq', right)  16.4 us
    dot_general x3, matrix products, attend(): jnp.einsum('hqk,khd->qhd', probs, values, preferred_element_type=jnp.floa...  13.2 us
    unnamed x25, local copies, waits for them, and re-layouts  12 us
  transfers between devices with their start and end apart: 10, of which 5 were waited for; matrix products, arithmetic and copies ran while one was open for 17% of the time, Pallas kernels for 0%

commit v1 on v0

--- a/solution.py
+++ b/solution.py
@@ -67,7 +67,10 @@
 
     blocks = lax.map(attend, jnp.arange(nodes // span, dtype=jnp.int32))
     attended = blocks.reshape(nodes, heads_here * HEAD_DIM)
-    node_attended = lax.all_to_all(attended, "seq", split_axis=0, concat_axis=1, tiled=True)
+    node_attended = jnp.concatenate(
+        lax.all_to_all(jnp.stack(jnp.split(attended, lax.axis_size("seq"), axis=0)), "seq", 0, 0),
+        axis=1,
+    )
     out_tiles = out_all
     attn_out = jnp.einsum(
         "nsk,sekc->nec",

time: 346 us -> 357 us (1.032)
  local copies, waits for them, and re-layouts: 59.7 us -> 68.1 us
    unnamed x25 -> x36, local copies, waits for them, and re-layouts: 12 us -> 21.3 us
    all_to_all x1, waiting for transfers between devices: 2.89 us -> 6.87 us  [per_device(): lax.all_to_all(jnp.stack(jnp.split(attended, lax.axis_size('seq'), axis=0...]
    all_gather x1 -> x0, local copies, waits for them, and re-layouts: 3.94 us -> none  [per_device(): out_all = lax.all_gather(out_rows[None], 'seq', axis=0, tiled=True)]
    reshape x0 -> x3, local copies, waits for them, and re-layouts: none -> 3.77 us  [the longest x2 2.51 us: per_device(): attended = blocks.reshape(nodes, heads_here * HEAD_DIM)]
  transfers between devices with their start and end apart: 10 -> 10, of which waited for: 5 -> 5; matrix products, arithmetic and copies ran while one was open for 17% -> 19% of each run, Pallas kernels for 0% -> 0%
where the time goes in v1:
time: 357 us; the launch traced here: 355 us
  blocking collectives  115 us (32%)
  waiting for transfers between devices  72.6 us (20%)
  local copies, waits for them, and re-layouts  68.1 us (19%)
  starting transfers between devices  40 us (11%)
  matrix products  33 us (9%)
  between operations  13.7 us (4%)
  other arithmetic  10.7 us (3%)
    all_to_all x1, blocking collectives, per_device(): lax.all_to_all(outgoing, ('seq', 'exp'), split_axis=0, concat_axis=0, til...  53 us
    all_to_all x1, waiting for transfers between devices, per_device(): lax.all_to_all(processed, ('seq', 'exp'), split_axis=0, concat_axis=0, ti...  50.2 us
    all_gather x1, blocking collectives, per_device(): out_rows = lax.all_gather(w_out[None], 'exp', axis=0, tiled=True)  33.4 us
    all_gather x1, blocking collectives, per_device(): cols_slice = lax.all_gather(w_qkv, 'exp', axis=0, tiled=True)  28.2 us
    unnamed x36, local copies, waits for them, and re-layouts  21.3 us
    ppermute x4, starting transfers between devices, per_device(): moving_r = lax.ppermute(moving_r, 'seq', right)  15.6 us
    ppermute x4, waiting for transfers between devices, per_device(): moving_r = lax.ppermute(moving_r, 'seq', right)  15.5 us
    dot_general x3, matrix products, attend(): jnp.einsum('hqk,khd->qhd', probs, values, preferred_element_type=jnp.floa...  13.2 us
  transfers between devices with their start and end apart: 10, of which 5 were waited for; matrix products, arithmetic and copies ran while one was open for 19% of the time, Pallas kernels for 0%

profile of v1, /device:TPU:26, one launch (start us, length us, event | category | flops | bytes accessed | tf_op | source)
XLA Modules:
  0.0 354.7 jit_solution(11602957375994477061)
XLA Ops:
  6.5 2.5 collective-permute-start
  9.0 4.7 %collective-permute-start.3 = (bf16[192,1024]{1,0:T(8,128)(2,1)}, bf16[192,1024]{1,0:T(8,128)(2,1)S(1)}, u32[]{:S(2)}, u32[]{:S(2)}) collective-permute-start(bf16[192,1024]{1,0:T(8,128)(2,1)} %bitcast.162), channel_id=1, source_target_pairs={{0,8},{8,16},{16,24},{24,32},{32,40},{40,48},{48,56},{56,0},{1,9},... | collective-permute-start | bytes 1179656 | tf_op jit(solution)/shard_map/ppermute | solution.py:31
  13.7 33.4 %all-gather = bf16[1024,128]{1,0:T(8,128)(2,1)} all-gather(bf16[128,128]{1,0:T(8,128)(2,1)} %param.14), channel_id=2, replica_groups=mesh['sub'=8,'seq'=8,'exp'=8] {'exp'}, dimensions={0}, use_global_device_ids=true | all-gather | bytes 294912 | tf_op jit(solution)/shard_map/all_gather | solution.py:22
  47.1 28.2 %all_gather.9 = bf16[1024,384]{1,0:T(8,128)(2,1)} all-gather(bf16[128,384]{1,0:T(8,128)(2,1)} %param.13), channel_id=1, replica_groups=mesh['sub'=8,'seq'=8,'exp'=8] {'exp'}, dimensions={0}, use_global_device_ids=true | all-gather | bytes 884736 | tf_op jit(solution)/shard_map/all_gather | solution.py:21
  75.4 3.5 collective-permute-start.4
  78.9 2.0 convert_bitcast_fusion
  80.8 2.3 collective-permute-start.1
  83.9 8.1 %collective-permute-done.4 = bf16[192,1024]{1,0:T(8,128)(2,1)} collective-permute-done((bf16[192,1024]{1,0:T(8,128)(2,1)S(1)}, bf16[192,1024]{1,0:T(8,128)(2,1)}, u32[]{:S(2)}, u32[]{:S(2)}) %collective-permute-start.4) | collective-permute-done | bytes 393248 | tf_op jit(solution)/shard_map/ppermute | solution.py:31
  92.0 3.5 collective-permute-start.5
  98.1 2.3 collective-permute-start.2
  100.4 1.8 bitcast_dynamic-update-slice_fusion.6
  102.2 3.9 %collective-permute-done.5 = bf16[192,1024]{1,0:T(8,128)(2,1)} collective-permute-done((bf16[192,1024]{1,0:T(8,128)(2,1)}, bf16[192,1024]{1,0:T(8,128)(2,1)}, u32[]{:S(2)}, u32[]{:S(2)}) %collective-permute-start.5) | collective-permute-done | bytes 393248 | tf_op jit(solution)/shard_map/ppermute | solution.py:31
  106.1 3.9 %collective-permute-start.6 = (bf16[192,1024]{1,0:T(8,128)(2,1)}, bf16[192,1024]{1,0:T(8,128)(2,1)S(1)}, u32[]{:S(2)}, u32[]{:S(2)}) collective-permute-start(bf16[192,1024]{1,0:T(8,128)(2,1)} %collective-permute-done.5), channel_id=1, source_target_pairs={{0,8},{8,16},{16,24},{24,32},{32,40},{40,48},{48,56},{56,0},{1,9},... | collective-permute-start | bytes 1179656 | tf_op jit(solution)/shard_map/ppermute | solution.py:31
  109.9 1.8 bitcast_dynamic-update-slice_fusion.5
  112.5 3.4 collective-permute-done.6
  116.7 1.8 bitcast_dynamic-update-slice_fusion.2
  118.5 1.8 bitcast_dynamic-update-slice_fusion.1
  121.0 4.3 %gather_fusion = bf16[8,192,1024]{2,1,0:T(8,128)(2,1)} fusion(bf16[8,192,1024]{2,1,0:T(8,128)(2,1)} %bitcast_dynamic-update-slice_fusion, s32[1024]{0:T(1024)S(1)} %pad_clamp_fusion.1), kind=kCustom, calls=%fused_computation | custom fusion | bytes 6291488 | tf_op jit(solution)/shard_map/jit(_take)/gather | solution.py:38
  125.4 2.4 bitcast_select_fusion
  127.8 1.4 convolution_convert_fusion
  130.2 27.9 %while.12 = (s32[]{:T(128)}, bf16[3,512,2,64]{1,3,2,0:T(8,128)(2,1)}, s32[3]{0:T(128)S(1)}, pred[12,1536]{1,0:T(8,128)(4,1)S(1)}, bf16[1536,2,64]{0,2,1:T(8,128)...) while((s32[]{:T(128)}, ...), condition=%wide.region_3.4_spmd, body=%wide.region_0.3_spmd.sunk | while | flops 618205184 | bytes 3959682 | solution.py:68
  131.7 3.4 fusion.90
  135.1 4.4 %fusion.91 = bf16[3,512,2,64]{1,3,2,0:T(8,128)(2,1)} fusion(bf16[3,512,2,64]{1,3,2,0:T(8,128)(2,1)} %get-tuple-element.176, s32[]{:T(128)} %get-tuple-element.175, bf16[1536,2,64]{0,2,1:T(8,128)(2,1)S(1)} %get-tuple-element.196, f32[2,512]{1,0:T(2,128)S(1)} %fusion.90, pred[512,1536]{1,0:T(8,128)(4,1)S(1)} %bitcast.159, ...), kind=kOutput, calls=%fused_computation.14.clone.1 | convolution fusion | flops 410585600 | bytes 1839620 | tf_op jit(solution)/shard_map/while/body/eval_jaxpr/hqk,khd->qhd/dot_general | solution.py:64
  141.0 3.4 fusion.90
  144.4 4.4 %fusion.91 = bf16[3,512,2,64]{1,3,2,0:T(8,128)(2,1)} fusion(bf16[3,512,2,64]{1,3,2,0:T(8,128)(2,1)} %get-tuple-element.176, s32[]{:T(128)} %get-tuple-element.175, bf16[1536,2,64]{0,2,1:T(8,128)(2,1)S(1)} %get-tuple-element.196, f32[2,512]{1,0:T(2,128)S(1)} %fusion.90, pred[512,1536]{1,0:T(8,128)(4,1)S(1)} %bitcast.159, ...), kind=kOutput, calls=%fused_computation.14.clone.1 | convolution fusion | flops 410585600 | bytes 1839620 | tf_op jit(solution)/shard_map/while/body/eval_jaxpr/hqk,khd->qhd/dot_general | solution.py:64
  150.3 3.4 fusion.90
  153.7 4.4 %fusion.91 = bf16[3,512,2,64]{1,3,2,0:T(8,128)(2,1)} fusion(bf16[3,512,2,64]{1,3,2,0:T(8,128)(2,1)} %get-tuple-element.176, s32[]{:T(128)} %get-tuple-element.175, bf16[1536,2,64]{0,2,1:T(8,128)(2,1)S(1)} %get-tuple-element.196, f32[2,512]{1,0:T(2,128)S(1)} %fusion.90, pred[512,1536]{1,0:T(8,128)(4,1)S(1)} %bitcast.159, ...), kind=kOutput, calls=%fused_computation.14.clone.1 | convolution fusion | flops 410585600 | bytes 1839620 | tf_op jit(solution)/shard_map/while/body/eval_jaxpr/hqk,khd->qhd/dot_general | solution.py:64
  158.1 2.2 copy.58
  162.0 1.5 fusion.60
  163.5 1.4 fusion.59
  166.3 1.4 fusion.57
  172.0 7.7 %all-to-all-start = ((bf16[8,192,128]{2,1,0:T(8,128)(2,1)}), bf16[8,192,128]{2,1,0:T(8,128)(2,1)S(1)}, u32[]{:S(2)}, u32[]{:S(2)}) async-start(bf16[8,192,128]{2,1,0:T(8,128)(2,1)} %fusion.54), calls=%async_computation | async-start | bytes 786432 | tf_op jit(solution)/shard_map/all_to_all | solution.py:71
  181.3 6.9 %all-to-all-done = bf16[8,192,128]{2,1,0:T(8,128)(2,1)S(1)} async-done(((bf16[8,192,128]{2,1,0:T(8,128)(2,1)}), bf16[8,192,128]{2,1,0:T(8,128)(2,1)S(1)}, u32[]{:S(2)}, u32[]{:S(2)}) %all-to-all-start) | async-done | bytes 393248 | tf_op jit(solution)/shard_map/all_to_all | solution.py:71
  188.9 2.6 fusion.44
  193.0 3.0 reshape.194
  196.0 4.0 %scatter_custom_fusion = bf16[768,1024]{1,0:T(8,128)(2,1)} fusion(s32[384]{0:T(512)S(1)} %fusion.62, bf16[384,1024]{1,0:T(8,128)(2,1)} %reshape.194, bf16[]{:T(256)} %constant.125.clone.1), kind=kCustom, calls=%fused_computation.50 | custom fusion | bytes 1573376 | tf_op jit(solution)/shard_map/scatter | solution.py:93
  199.9 3.6 %reshape.168 = bf16[64,12,1024]{2,1,0:T(8,128)(2,1)} reshape(bf16[768,1024]{1,0:T(8,128)(2,1)} %scatter_custom_fusion) | data formatting | bytes 3145728 | tf_op jit(solution)/shard_map/reshape | solution.py:95
  203.6 53.0 %all_to_all.15 = bf16[64,12,1024]{2,1,0:T(8,128)(2,1)} all-to-all(bf16[64,12,1024]{2,1,0:T(8,128)(2,1)} %reshape.168), channel_id=1, replica_groups=mesh['sub'=8,'seq'=8,'exp'=8] {'seq','exp'}, dimensions={0} | all-to-all | bytes 3145728 | tf_op jit(solution)/shard_map/all_to_all | solution.py:97
  256.6 3.6 %reshape.169 = bf16[768,1024]{1,0:T(8,128)(2,1)} reshape(bf16[64,12,1024]{2,1,0:T(8,128)(2,1)} %all_to_all.15) | data formatting | bytes 3145728 | tf_op jit(solution)/shard_map/reshape | solution.py:99
  260.2 3.3 fusion.33
  263.5 2.2 convolution_convert_fusion.1
  265.7 3.6 %reshape.170 = bf16[64,12,1024]{2,1,0:T(8,128)(2,1)} reshape(bf16[768,1024]{1,0:T(8,128)(2,1)} %convolution_convert_fusion.1) | data formatting | bytes 3145728 | tf_op jit(solution)/shard_map/reshape | solution.py:103
  269.3 9.6 %all-to-all-start.2 = ((bf16[64,12,1024]{2,1,0:T(8,128)(2,1)}), bf16[64,12,1024]{2,1,0:T(8,128)(2,1)}, u32[]{:S(2)}, u32[]{:S(2)}) async-start(bf16[64,12,1024]{2,1,0:T(8,128)(2,1)} %reshape.170), calls=%async_computation.2 | async-start | bytes 4194304 | tf_op jit(solution)/shard_map/all_to_all | solution.py:104
  281.7 50.2 %all-to-all-done.2 = bf16[64,12,1024]{2,1,0:T(8,128)(2,1)} async-done(((bf16[64,12,1024]{2,1,0:T(8,128)(2,1)}), bf16[64,12,1024]{2,1,0:T(8,128)(2,1)}, u32[]{:S(2)}, u32[]{:S(2)}) %all-to-all-start.2) | async-done | bytes 1572896 | tf_op jit(solution)/shard_map/all_to_all | solution.py:104
  331.9 3.6 %reshape.171 = bf16[768,1024]{1,0:T(8,128)(2,1)} reshape(bf16[64,12,1024]{2,1,0:T(8,128)(2,1)} %all-to-all-done.2) | data formatting | bytes 3145728 | tf_op jit(solution)/shard_map/reshape | solution.py:106
  335.5 5.0 %gather_fusion.1 = bf16[384,1024]{1,0:T(8,128)(2,1)} fusion(bf16[768,1024]{1,0:T(8,128)(2,1)} %reshape.171, s32[1024]{0:T(1024)S(1)} %pad_clamp_fusion), kind=kCustom, calls=%fused_computation.1 | custom fusion | bytes 1574400 | tf_op jit(solution)/shard_map/gather | solution.py:107
  340.5 3.0 reshape.173
  343.5 3.4 multiply_reduce_fusion
  (77 shorter events, 23.8 us)
Async XLA Ops:
  6.5 253.7 %copy-start = (bf16[1,1024,1024]{2,1,0:T(8,128)(2,1)S(1)}, bf16[1,1024,1024]{2,1,0:T(8,128)(2,1)}, u32[]{:S(2)}) copy-start(bf16[1,1024,1024]{2,1,0:T(8,128)(2,1)} %param.18) | copy-start | bytes 6291460
  6.5 181.6 %all-gather.4.cloned.1.call-start = ((), (), s32[]{:S(2)}) async-start(), calls=%async_computation.3 | async-start | bytes 2359296 | tf_op jit(solution)/shard_map/all_gather | solution.py:23
  6.5 74.3 %collective-permute-start = (bf16[192,1024]{1,0:T(8,128)(2,1)}, bf16[192,1024]{1,0:T(8,128)(2,1)}, u32[]{:S(2)}, u32[]{:S(2)}) collective-permute-start(bf16[192,1024]{1,0:T(8,128)(2,1)} %bitcast.161), channel_id=1, source_target_pairs={{0,56},{8,0},{16,8},{24,16},{32,24},{40,32},{48,40},{56,48},{1,57}... | collective-permute-start | bytes 1179656 | tf_op jit(solution)/shard_map/ppermute | solution.py:34
  9.0 66.3 %collective-permute-start.3 = (bf16[192,1024]{1,0:T(8,128)(2,1)}, bf16[192,1024]{1,0:T(8,128)(2,1)S(1)}, u32[]{:S(2)}, u32[]{:S(2)}) collective-permute-start(bf16[192,1024]{1,0:T(8,128)(2,1)} %bitcast.162), channel_id=1, source_target_pairs={{0,8},{8,16},{16,24},{24,32},{32,40},{40,48},{48,56},{56,0},{1,9},... | collective-permute-start | bytes 1179656 | tf_op jit(solution)/shard_map/ppermute | solution.py:31
  75.4 16.7 %collective-permute-start.4 = (bf16[192,1024]{1,0:T(8,128)(2,1)S(1)}, bf16[192,1024]{1,0:T(8,128)(2,1)}, u32[]{:S(2)}, u32[]{:S(2)}) collective-permute-start(bf16[192,1024]{1,0:T(8,128)(2,1)S(1)} %collective-permute-done.3), channel_id=1, source_target_pairs={{0,8},{8,16},{16,24},{24,32},{32,40},{40,48},{48,56},{56,0},{1,9},... | collective-permute-start | bytes 1179656 | tf_op jit(solution)/shard_map/ppermute | solution.py:31
  80.8 17.2 %collective-permute-start.1 = (bf16[192,1024]{1,0:T(8,128)(2,1)}, bf16[192,1024]{1,0:T(8,128)(2,1)}, u32[]{:S(2)}, u32[]{:S(2)}) collective-permute-start(bf16[192,1024]{1,0:T(8,128)(2,1)} %collective-permute-done), channel_id=1, source_target_pairs={{0,56},{8,0},{16,8},{24,16},{32,24},{40,32},{48,40},{56,48},{1,57}... | collective-permute-start | bytes 1179656 | tf_op jit(solution)/shard_map/ppermute | solution.py:34
  92.0 14.1 %collective-permute-start.5 = (bf16[192,1024]{1,0:T(8,128)(2,1)}, bf16[192,1024]{1,0:T(8,128)(2,1)}, u32[]{:S(2)}, u32[]{:S(2)}) collective-permute-start(bf16[192,1024]{1,0:T(8,128)(2,1)} %collective-permute-done.4), channel_id=1, source_target_pairs={{0,8},{8,16},{16,24},{24,32},{32,40},{40,48},{48,56},{56,0},{1,9},... | collective-permute-start | bytes 1179656 | tf_op jit(solution)/shard_map/ppermute | solution.py:31
  98.1 13.6 %collective-permute-start.2 = (bf16[192,1024]{1,0:T(8,128)(2,1)}, bf16[192,1024]{1,0:T(8,128)(2,1)S(1)}, u32[]{:S(2)}, u32[]{:S(2)}) collective-permute-start(bf16[192,1024]{1,0:T(8,128)(2,1)} %collective-permute-done.1), channel_id=1, source_target_pairs={{0,56},{8,0},{16,8},{24,16},{32,24},{40,32},{48,40},{56,48},{1,57}... | collective-permute-start | bytes 1179656 | tf_op jit(solution)/shard_map/ppermute | solution.py:34
  106.1 9.9 %collective-permute-start.6 = (bf16[192,1024]{1,0:T(8,128)(2,1)}, bf16[192,1024]{1,0:T(8,128)(2,1)S(1)}, u32[]{:S(2)}, u32[]{:S(2)}) collective-permute-start(bf16[192,1024]{1,0:T(8,128)(2,1)} %collective-permute-done.5), channel_id=1, source_target_pairs={{0,8},{8,16},{16,24},{24,32},{32,40},{40,48},{48,56},{56,0},{1,9},... | collective-permute-start | bytes 1179656 | tf_op jit(solution)/shard_map/ppermute | solution.py:31
  125.4 2.4 copy-start.4
  158.1 22.8 %copy-start.5 = (s32[1,192,2]{1,2,0:T(2,128)S(1)}, s32[1,192,2]{1,2,0:T(2,128)}, u32[]{:S(2)}) copy-start(s32[1,192,2]{1,2,0:T(2,128)} %param.16) | copy-start | bytes 4612
  160.6 0.7 copy-start.3
  162.0 29.5 %copy-start.1 = (bf16[1,192,1024]{2,1,0:T(8,128)(2,1)S(1)}, bf16[1,192,1024]{2,1,0:T(8,128)(2,1)}, u32[]{:S(2)}) copy-start(bf16[1,192,1024]{2,1,0:T(8,128)(2,1)} %param.11) | copy-start | bytes 1179652
  162.0 29.5 %copy-start.6 = (f32[1024]{0:T(1024)S(1)}, f32[1024]{0:T(1024)}, u32[]{:S(2)}) copy-start(f32[1024]{0:T(1024)} %param.15) | copy-start | bytes 12292
  172.0 16.2 %all-to-all-start = ((bf16[8,192,128]{2,1,0:T(8,128)(2,1)}), bf16[8,192,128]{2,1,0:T(8,128)(2,1)S(1)}, u32[]{:S(2)}, u32[]{:S(2)}) async-start(bf16[8,192,128]{2,1,0:T(8,128)(2,1)} %fusion.54), calls=%async_computation | async-start | bytes 786432 | tf_op jit(solution)/shard_map/all_to_all | solution.py:71
  188.2 0.7 copy-start.2
  260.2 3.3 copy-start.8
  265.7 13.3 %copy-start.7 = (f32[1,192,2]{1,2,0:T(2,128)S(1)}, f32[1,192,2]{1,2,0:T(2,128)}, u32[]{:S(2)}) copy-start(f32[1,192,2]{1,2,0:T(2,128)} %param.17) | copy-start | bytes 4612
  269.3 62.6 %all-to-all-start.2 = ((bf16[64,12,1024]{2,1,0:T(8,128)(2,1)}), bf16[64,12,1024]{2,1,0:T(8,128)(2,1)}, u32[]{:S(2)}, u32[]{:S(2)}) async-start(bf16[64,12,1024]{2,1,0:T(8,128)(2,1)} %reshape.170), calls=%async_computation.2 | async-start | bytes 4194304 | tf_op jit(solution)/shard_map/all_to_all | solution.py:104
Sparse Core Ops, SparseCore 0:
  47.2 42.2 all-gather.3
